TPU v7x, 32 devices: a whole 2x2x4 slice. The times are simulated.
32 devices in a mesh: gx: 8 (over z, y), gy: 4 (over x, core).
Axes of the slice: x: 2, y: 2, z: 4, core: 2. Of those that a mesh axis runs over, the one named last changes fastest.
Arguments:
- conc_prev: float32 [128, 64, 128], P('gx', 'gy'), may hold values from 0.5 to 2
- right_side: float32 [128, 64, 128], P('gx', 'gy'), may hold values from -5 to 7
- soil_id: int32 [128, 64, 128], P('gx', 'gy'), may hold values from 0 to 7
- soil_table: float32 [5, 8], replicated, may hold values from 0.3 to 3
Outputs:
- correction: float32 [128, 64, 128], P('gx', 'gy')
All inputs are finite; a program needn't handle non-finite values.
Results may differ from a plain program's by a relative error of at most 0.00002.
Values sent between devices are 32-bit elements; how exact they have to be, the bound alone decides.
No kernel may reach another device: no remote copies, remote signals or barrier semaphores. Data moves between devices by JAX's collectives and lax.ppermute only.
A program may use at most 128 MiB of HBM per device.

v0:
```python
import jax
import jax.numpy as jnp
from jax import lax
from jax.sharding import PartitionSpec as P

CHEB = 3
COARSE_SWEEPS = 8
storage_scale = 0.05
cheb_centre = 1.1
cheb_half = 0.9
cheb_ratio = cheb_centre / cheb_half
jacobi_weight = 0.8
FINE_HALO = 10
MID_HALO = 5
HIGH = lax.Precision.HIGHEST


def shift_from(cells, axis, offset):
    count = lax.axis_size(axis)
    if offset > 0:
        pairs = [(i + offset, i) for i in range(count - offset)]
    else:
        pairs = [(i, i - offset) for i in range(count + offset)]
    if not pairs:
        return jnp.zeros_like(cells)
    return lax.ppermute(cells, axis, pairs)


def halo(cells, sides, width):
    for axis, dim in sides:
        size = cells.shape[dim]
        head = lax.slice_in_dim(cells, 0, width, axis=dim)
        tail = lax.slice_in_dim(cells, size - width, size, axis=dim)
        cells = jnp.concatenate(
            [shift_from(tail, axis, -1), cells, shift_from(head, axis, 1)], axis=dim
        )
    return cells


def harmonic(first, second):
    return first * second / jnp.maximum(0.5 * (first + second), 0.1)


def win(a, n, margin, r, dx=0, dy=0):
    lo = margin - r
    hi = margin + n + r
    return a[..., lo + dx : hi + dx, lo + dy : hi + dy, :]


def pair_matrix(size, dtype=jnp.float32):
    rows = jnp.arange(size)[:, None] // 2
    cols = jnp.arange(size // 2)[None, :]
    return (rows == cols).astype(dtype)


def coarsen(values):
    lead = values.shape[:-3]
    sx, sy, sz = values.shape[-3:]
    v = values.reshape(lead + (sx // 2, 2, sy, sz))
    v = v[..., 0, :, :] + v[..., 1, :, :]
    v = jnp.einsum("...yz,zw->...yw", v, pair_matrix(sz), precision=HIGH)
    v = jnp.einsum("...yw,yv->...vw", v, pair_matrix(sy), precision=HIGH)
    return v * 0.125


def prolong(values):
    sx, sy, sz = values.shape
    v = jnp.einsum("xyz,wz->xyw", values, pair_matrix(2 * sz), precision=HIGH)
    v = jnp.einsum("xyw,vy->xvw", v, pair_matrix(2 * sy), precision=HIGH)
    v = jnp.broadcast_to(v[:, None], (sx, 2) + v.shape[1:]).reshape((2 * sx,) + v.shape[1:])
    return v


def build_level(coeffs, n, margin, spacing):
    kx, ky, kz, store = (coeffs[0], coeffs[1], coeffs[2], coeffs[3])
    fx = harmonic(kx[1:], kx[:-1]) * spacing
    fy = harmonic(ky[:, 1:], ky[:, :-1]) * spacing
    vertical = harmonic(kz[:, :, 1:], kz[:, :, :-1]) * spacing
    closed = jnp.zeros_like(kz[:, :, :1])
    above = jnp.concatenate([vertical, closed], axis=2)
    below = jnp.concatenate([closed, vertical], axis=2)
    level = dict(n=n, m=margin, fx=fx, fy=fy, above=above, below=below, store=store)
    r = margin - 1
    level["diag"] = jnp.maximum(faces_sum(level, r) + win(store, n, margin, r), 0.01)
    level["dm"] = r
    return level


def faces_sum(level, r):
    n, m = (level["n"], level["m"])
    east = win(level["fx"], n, m, r)
    west = win(level["fx"], n, m, r, dx=-1)
    north = win(level["fy"], n, m, r)
    south = win(level["fy"], n, m, r, dy=-1)
    above = win(level["above"], n, m, r)
    below = win(level["below"], n, m, r)
    return east + west + north + south + above + below


def operate(values, vm, level):
    n, m = (level["n"], level["m"])
    r = vm - 1
    centre = win(values, n, vm, r)
    upper = jnp.concatenate([centre[:, :, 1:], centre[:, :, :1]], axis=2)
    lower = jnp.concatenate([centre[:, :, -1:], centre[:, :, :-1]], axis=2)
    fx, fy = (level["fx"], level["fy"])
    fluxes = win(fx, n, m, r) * (centre - win(values, n, vm, r, dx=1))
    fluxes = fluxes + win(fx, n, m, r, dx=-1) * (centre - win(values, n, vm, r, dx=-1))
    fluxes = fluxes + win(fy, n, m, r) * (centre - win(values, n, vm, r, dy=1))
    fluxes = fluxes + win(fy, n, m, r, dy=-1) * (centre - win(values, n, vm, r, dy=-1))
    fluxes = fluxes + win(level["above"], n, m, r) * (centre - upper)
    fluxes = fluxes + win(level["below"], n, m, r) * (centre - lower)
    return win(level["store"], n, m, r) * centre + fluxes


def chebyshev(target, tm, initial, im, level):
    n = level["n"]
    diag, dm = (level["diag"], level["dm"])
    if initial is None:
        cur = min(tm, dm)
        misfit = win(target, n, tm, cur)
        update = misfit / win(diag, n, dm, cur) * (1.0 / cheb_centre)
        iterate = update
    else:
        applied = operate(initial, im, level)
        cur = im - 1
        misfit = win(target, n, tm, cur) - applied
        update = misfit / win(diag, n, dm, cur) * (1.0 / cheb_centre)
        iterate = win(initial, n, im, cur) + update
    factor = 1.0 / cheb_ratio
    for repeat in range(CHEB - 1):
        applied = operate(iterate, cur, level)
        nxt = cur - 1
        misfit = win(target, n, tm, nxt) - applied
        factor_new = 1.0 / (2.0 * cheb_ratio - factor)
        update = factor_new * factor * win(update, n, cur, nxt) + 2.0 * factor_new / cheb_half * (
            misfit / win(diag, n, dm, nxt)
        )
        iterate = win(iterate, n, cur, nxt) + update
        cur = nxt
        factor = factor_new
    return (iterate, cur)


def lookup(soil_id, soil_table, record):
    looked = jnp.full(soil_id.shape, soil_table[record, soil_table.shape[1] - 1])
    for material in range(soil_table.shape[1] - 2, -1, -1):
        looked = jnp.where(soil_id == material, soil_table[record, material], looked)
    return looked


def local(conc_prev, right_side, soil_id, soil_table):
    n = conc_prev.shape[0]
    ny = conc_prev.shape[1]
    hf = FINE_HALO
    gx_count = lax.axis_size("gx")
    gy_count = lax.axis_size("gy")
    ix = lax.axis_index("gx")
    iy = lax.axis_index("gy")
    stacked = jnp.stack([conc_prev, right_side, soil_id.astype(jnp.float32)])
    ext = halo(stacked, (("gx", 1), ("gy", 2)), hf)
    conc, rhs, idf = (ext[0], ext[1], ext[2])
    ids = idf.astype(jnp.int32)
    gxi = ix * n - hf + jnp.arange(n + 2 * hf)
    gyi = iy * ny - hf + jnp.arange(ny + 2 * hf)
    inside = ((gxi >= 0) & (gxi < gx_count * n))[:, None, None] & (
        (gyi >= 0) & (gyi < gy_count * ny)
    )[None, :, None]
    kx = jnp.where(inside, lookup(ids, soil_table, 0), 0.0)
    ky = jnp.where(inside, lookup(ids, soil_table, 1), 0.0)
    kz = jnp.where(inside, lookup(ids, soil_table, 2), 0.0)
    s3 = lookup(ids, soil_table, 3)
    s4 = lookup(ids, soil_table, 4)
    store = storage_scale * (1.0 + s3 * jnp.exp((s4 - 1.0) * jnp.log(conc)))
    store = jnp.where(inside, store, 0.0)
    fine_c = jnp.stack([kx, ky, kz, store])
    fine = build_level(fine_c, n, hf, 1.0)
    x0, x0m = chebyshev(rhs, hf, None, 0, fine)
    r0 = win(rhs, n, hf, x0m - 1) - operate(x0, x0m, fine)
    r0m = x0m - 1
    nm = n // 2
    mm = hf // 2
    mid_c = coarsen(fine_c)
    mid = build_level(mid_c, nm, mm, 0.25)
    b1 = coarsen(win(r0, n, r0m, 2 * (r0m // 2)))
    b1m = r0m // 2
    x1, x1m = chebyshev(b1, b1m, None, 0, mid)
    r1 = win(b1, nm, b1m, x1m - 1) - operate(x1, x1m, mid)
    r1m = x1m - 1
    b2 = coarsen(win(r1, nm, r1m, 0))
    coarse_own = coarsen(win(mid_c, nm, mm, 0))
    nc = b2.shape[0]
    reach = 2
    cpack = jnp.concatenate([b2[None], coarse_own], axis=0)
    cpack = lax.all_gather(cpack, "gy", axis=2, tiled=True)
    parts = [shift_from(cpack, "gx", -d) for d in range(reach, 0, -1)]
    parts += [cpack]
    parts += [shift_from(cpack, "gx", d) for d in range(1, reach + 1)]
    cpack = jnp.concatenate(parts, axis=1)
    cm = reach * nc
    source = cpack[0]
    cc = cpack[1:]
    line_total = jnp.sum(source, axis=1)
    line_store = jnp.sum(cc[3], axis=1)
    line_mean = jnp.where(
        line_store > 0, line_total / jnp.where(line_store > 0, line_store, 1.0), 0.0
    )
    width = source.shape[0]
    ccp = jnp.pad(cc, ((0, 0), (0, 0), (1, 1), (0, 0)))
    kx_, ky_, kz_, st_ = (ccp[0], ccp[1], ccp[2], ccp[3])
    q = 0.0625
    cx = kx_[1:-1, 1:-1]
    cy = ky_[1:-1, 1:-1]
    cz = kz_[1:-1, 1:-1]
    east = harmonic(kx_[2:, 1:-1], cx) * q
    west = harmonic(kx_[:-2, 1:-1], cx) * q
    north = harmonic(ky_[1:-1, 2:], cy) * q
    south = harmonic(ky_[1:-1, :-2], cy) * q
    vert = harmonic(cz[:, :, 1:], cz[:, :, :-1]) * q
    closed = jnp.zeros_like(cz[:, :, :1])
    above = jnp.concatenate([vert, closed], axis=2)
    below = jnp.concatenate([closed, vert], axis=2)
    cst = st_[1:-1, 1:-1]
    cdiag = jnp.maximum(cst + east + west + north + south + above + below, 0.01)
    csrc = source[1:-1]
    u = jnp.broadcast_to(line_mean[:, None, :], source.shape)
    for sweep in range(COARSE_SWEEPS):
        lo = sweep
        cur = u
        up = jnp.pad(cur, ((0, 0), (1, 1), (0, 0)))
        centre = up[1:-1, 1:-1]
        sl = slice(lo, width - 2 - lo)
        upper = jnp.concatenate([centre[:, :, 1:], centre[:, :, :1]], axis=2)
        lower = jnp.concatenate([centre[:, :, -1:], centre[:, :, :-1]], axis=2)
        fl = east[sl] * (centre - up[2:, 1:-1]) + west[sl] * (centre - up[:-2, 1:-1])
        fl = fl + north[sl] * (centre - up[1:-1, 2:]) + south[sl] * (centre - up[1:-1, :-2])
        fl = fl + above[sl] * (centre - upper) + below[sl] * (centre - lower)
        applied = cst[sl] * centre + fl
        u = centre + jacobi_weight * ((csrc[sl] - applied) / cdiag[sl])
    ncy = nc
    u = lax.dynamic_slice_in_dim(u, iy * ncy, ncy, 1)
    s1 = win(x1, nm, x1m, 0) + prolong(u)
    mpack = jnp.stack([s1, win(b1, nm, b1m, 0)])
    mpack = halo(mpack, (("gx", 1), ("gy", 2)), MID_HALO)
    s1e, b1e = (mpack[0], mpack[1])
    y1, y1m = chebyshev(b1e, MID_HALO, s1e, MID_HALO, mid)
    fm = 2 * y1m
    s0 = win(x0, n, x0m, fm) + prolong(y1)
    fs = min(fm, CHEB)
    s0 = win(s0, n, fm, fs)
    out, om = chebyshev(rhs, hf, s0, fs, fine)
    return out


def solution(mesh):
    placed = (P("gx", "gy", None), P("gx", "gy", None), P("gx", "gy", None), P())
    return jax.shard_map(
        local, mesh=mesh, in_specs=placed, out_specs=P("gx", "gy", None), check_vma=False
    )
```

profile of v0, /device:TPU:1, one launch (start us, length us, event | category | flops | bytes accessed | tf_op | source)
XLA Modules:
  0.0 162.3 jit_solution(11000969976232683504)
XLA Ops:
  2.1 4.0 %collective-permute-start = (f32[3,10,16,128]{3,1,2,0:T(8,128)S(1)}, f32[3,10,16,128]{3,1,2,0:T(8,128)S(1)}, u32[]{:S(2)}, u32[]{:S(2)}) collective-permute-start(f32[3,10,16,128]{3,1,2,0:T(8,128)S(1)} %get-tuple-element.62), channel_id=1, source_target_pairs={{0,4},{4,8},{8,12},{12,16},{16,20},{20,24},{24,28},{1,5},{5,9},{9,... | collective-permute-start | bytes 737288 | tf_op jit(solution)/shard_map/ppermute | solution.py:26
  6.1 1.3 collective-permute-start.1
  9.2 13.1 %collective-permute-done = f32[3,10,16,128]{3,1,2,0:T(8,128)S(1)} collective-permute-done((f32[3,10,16,128]{3,1,2,0:T(8,128)S(1)}, f32[3,10,16,128]{3,1,2,0:T(8,128)S(1)}, u32[]{:S(2)}, u32[]{:S(2)}) %collective-permute-start) | collective-permute-done | bytes 245792 | tf_op jit(solution)/shard_map/ppermute | solution.py:26
  22.5 4.6 %collective-permute-start.2 = (f32[3,36,10,128]{3,1,2,0:T(8,128)S(1)}, f32[3,36,10,128]{3,1,2,0:T(8,128)S(1)}, u32[]{:S(2)}, u32[]{:S(2)}) collective-permute-start(f32[3,36,10,128]{3,1,2,0:T(8,128)S(1)} %get-tuple-element.37), channel_id=1, source_target_pairs={{0,1},{1,2},{2,3},{4,5},{5,6},{6,7},{8,9},{9,10},{10,11},{12,13},{... | collective-permute-start | bytes 1658888 | tf_op jit(solution)/shard_map/ppermute | solution.py:26
  27.1 1.9 %collective-permute-start.3 = (f32[3,36,10,128]{3,1,2,0:T(8,128)S(1)}, f32[3,36,10,128]{3,1,2,0:T(8,128)S(1)}, u32[]{:S(2)}, u32[]{:S(2)}) collective-permute-start(f32[3,36,10,128]{3,1,2,0:T(8,128)S(1)} %get-tuple-element.38), channel_id=1, source_target_pairs={{1,0},{2,1},{3,2},{5,4},{6,5},{7,6},{9,8},{10,9},{11,10},{13,12},{... | collective-permute-start | bytes 1658888 | tf_op jit(solution)/shard_map/ppermute | solution.py:26
  30.5 3.6 %collective-permute-done.2 = f32[3,36,10,128]{3,1,2,0:T(8,128)S(1)} collective-permute-done((f32[3,36,10,128]{3,1,2,0:T(8,128)S(1)}, f32[3,36,10,128]{3,1,2,0:T(8,128)S(1)}, u32[]{:S(2)}, u32[]{:S(2)}) %collective-permute-start.2) | collective-permute-done | bytes 552992 | tf_op jit(solution)/shard_map/ppermute | solution.py:26
  34.1 4.4 %collective-permute-done.3 = f32[3,36,10,128]{3,1,2,0:T(8,128)S(1)} collective-permute-done((f32[3,36,10,128]{3,1,2,0:T(8,128)S(1)}, f32[3,36,10,128]{3,1,2,0:T(8,128)S(1)}, u32[]{:S(2)}, u32[]{:S(2)}) %collective-permute-start.3) | collective-permute-done | bytes 552992 | tf_op jit(solution)/shard_map/ppermute | solution.py:26
  38.7 6.1 %broadcast_select_fusion.3 = (f32[1,36,36,128]{3,1,2,0:T(8,128)S(1)}, pred[1,36,36,128]{3,1,2,0:T(8,128)(4,1)S(1)}, pred[1,36,36,128]{3,1,2,0:T(8,128)(4,1)S(1)}...) fusion(pred[36,36]{0,1:T(8,128)(4,1)S(1)} %broadcast_and_fusion, ...), kind=kLoop, calls=%fused_computation.137 | loop fusion | flops 2654208 | bytes 3816752 | tf_op jit(solution)/shard_map/jit(_where)/select_n | solution.py:169
  44.8 5.5 %broadcast_select_fusion.2 = f32[1,36,36,128]{3,1,2,0:T(8,128)S(1)} fusion(pred[36,36]{0,1:T(8,128)(4,1)S(1)} %broadcast_and_fusion, pred[1,36,36,128]{3,1,2,0:T(8,128)(4,1)S(1)} %get-tuple-element.33, pred[1,36,36,128]{3,1,2,0:T(8,128)(4,1)S(1)} %get-tuple-element.32, pred[1,36,36,128]{3,1,2,0:T(8,128)(4,1)S(1)} %get-tuple-element.31, ...), kind=kLoop, calls=%fused_computation.136 | loop fusion | flops 1327104 | bytes 1826096 | tf_op jit(solution)/shard_map/jit(_where)/select_n | solution.py:170
  50.3 5.5 %bitcast_select_fusion.2 = f32[36,36,128]{2,0,1:T(8,128)S(1)} fusion(pred[36,36]{0,1:T(8,128)(4,1)S(1)} %broadcast_and_fusion, pred[1,36,36,128]{3,1,2,0:T(8,128)(4,1)S(1)} %get-tuple-element.33, pred[1,36,36,128]{3,1,2,0:T(8,128)(4,1)S(1)} %get-tuple-element.32, pred[1,36,36,128]{3,1,2,0:T(8,128)(4,1)S(1)} %get-tuple-element.31, ...), kind=kLoop, calls=%fused_computation.31 | loop fusion | flops 1327104 | bytes 1826096 | tf_op jit(solution)/shard_map/jit(_where)/select_n | solution.py:170
  55.8 5.7 %broadcast_select_fusion.1 = f32[1,36,36,128]{3,1,2,0:T(8,128)S(1)} fusion(pred[36,36]{0,1:T(8,128)(4,1)S(1)} %broadcast_and_fusion, pred[1,36,36,128]{3,1,2,0:T(8,128)(4,1)S(1)} %get-tuple-element.33, pred[1,36,36,128]{3,1,2,0:T(8,128)(4,1)S(1)} %get-tuple-element.32, pred[1,36,36,128]{3,1,2,0:T(8,128)(4,1)S(1)} %get-tuple-element.31, ...), kind=kLoop, calls=%fused_computation.135 | loop fusion | flops 1327104 | bytes 1826096 | tf_op jit(solution)/shard_map/jit(_where)/select_n | solution.py:171
  61.5 5.7 %bitcast_select_fusion.1 = f32[36,36,128]{2,0,1:T(8,128)S(1)} fusion(pred[36,36]{0,1:T(8,128)(4,1)S(1)} %broadcast_and_fusion, pred[1,36,36,128]{3,1,2,0:T(8,128)(4,1)S(1)} %get-tuple-element.33, pred[1,36,36,128]{3,1,2,0:T(8,128)(4,1)S(1)} %get-tuple-element.32, pred[1,36,36,128]{3,1,2,0:T(8,128)(4,1)S(1)} %get-tuple-element.31, ...), kind=kLoop, calls=%fused_computation.30 | loop fusion | flops 1327104 | bytes 1826096 | tf_op jit(solution)/shard_map/jit(_where)/select_n | solution.py:171
  68.0 11.0 %broadcast_select_fusion = (f32[1,36,36,128]{3,1,2,0:T(8,128)S(1)}, f32[1,36,36,128]{3,1,2,0:T(8,128)S(1)}) fusion(pred[36,36]{0,1:T(8,128)(4,1)S(1)} %broadcast_and_fusion, f32[3,36,36,128]{3,1,2,0:T(8,128)S(1)} %pad_maximum_fusion.1, pred[1,36,36,128]{3,1,2,0:T(8,128)(4,1)S(1)} %get-tuple-element.33, pred[1,36,36,128]{3,1,2,0:T(8,128)(4,1)S(1)} %get-tuple-element.32, ...), kind=kLoop, calls=%fused_computation.134 | loop fusion | flops 3317760 | bytes 3153232 | tf_op jit(solution)/shard_map/jit(_where)/select_n | solution.py:175
  81.1 2.7 %pad_maximum_fusion = f32[4,18,2,36,128]{4,0,3,2,1:T(4,128)S(1)} fusion(f32[1,18,2,36,128]{4,0,3,2,1:T(1,128)S(1)} %bitcast.252, f32[1,18,2,36,128]{4,0,3,2,1:T(1,128)S(1)} %bitcast.254, f32[1,18,2,36,128]{4,0,3,2,1:T(1,128)S(1)} %bitcast.253, f32[1,18,2,36,128]{4,0,3,2,1:T(1,128)S(1)} %bitcast.251), kind=kLoop, calls=%fused_computation | loop fusion | flops 1990656 | bytes 5308416 | tf_op jit(solution)/shard_map/stack | solution.py:176
  87.3 5.6 %bitcast_select_fusion.3 = (f32[36,36,128]{2,0,1:T(8,128)S(1)}, f32[36,36,128]{2,0,1:T(8,128)S(1)}) fusion(pred[36,36]{0,1:T(8,128)(4,1)S(1)} %broadcast_and_fusion, pred[1,36,36,128]{3,1,2,0:T(8,128)(4,1)S(1)} %get-tuple-element.33, pred[1,36,36,128]{3,1,2,0:T(8,128)(4,1)S(1)} %get-tuple-element.32, pred[1,36,36,128]{3,1,2,0:T(8,128)(4,1)S(1)} %get-tuple-element.31, ...), kind=kLoop, calls=%fused_computation.32 | loop fusion | flops 1492992 | bytes 3153200 | tf_op jit(solution)/shard_map/jit(_where)/select_n | solution.py:169
  94.6 1.2 slice_add_fusion.5
  99.4 1.7 %fusion.58 = f32[28,28,128]{2,0,1:T(8,128)} fusion(f32[36,36,127]{2,0,1:T(8,128)S(1)} %maximum_divide_fusion, f32[30,30,128]{2,0,1:T(8,128)S(1)} %fusion.33, f32[36,35,128]{2,0,1:T(8,128)S(1)} %maximum_divide_fusion.2, f32[35,36,128]{2,0,1:T(8,128)S(1)} %maximum_divide_fusion.1, f32[36,36,128]{2,0,1:T(8,128)S(1)} %get-tuple-element.151, ...), kind=kLoop, calls=%fused_computation.116 | loop fusion | flops 2207744 | bytes 6278080 | tf_op jit(solution)/shard_map/sub | solution.py:179
  101.1 2.0 %reshape.377 = f32[14,2,28,128]{3,1,0,2:T(2,128)} reshape(f32[28,28,128]{2,0,1:T(8,128)} %fusion.58) | data formatting | bytes 802816 | tf_op jit(solution)/shard_map/reshape | solution.py:59
  103.1 1.5 fusion.426
  105.5 1.5 add_maximum_fusion.1
  109.1 4.4 %all_gather.3 = f32[5,4,16,32]{3,1,0,2:T(4,128)S(1)} all-gather(f32[5,4,4,32]{3,1,0,2:T(4,128)S(1)} %copy.39), channel_id=1, replica_groups=mesh['gx'=8,'gy'=4] {'gy'}, dimensions={2}, use_global_device_ids=true | all-gather | bytes 51200 | tf_op jit(solution)/shard_map/all_gather | solution.py:195
  113.4 5.1 %collective-permute-start.4 = (f32[5,4,16,32]{3,2,1,0:T(8,128)S(1)}, f32[5,4,16,32]{3,2,1,0:T(8,128)S(1)}, u32[]{:S(2)}, u32[]{:S(2)}) collective-permute-start(f32[5,4,16,32]{3,2,1,0:T(8,128)S(1)} %copy.40), channel_id=1, source_target_pairs={{0,8},{4,12},{8,16},{12,20},{16,24},{20,28},{1,9},{5,13},{9,17},{1... | collective-permute-start | bytes 122888 | tf_op jit(solution)/shard_map/ppermute | solution.py:26
  118.5 1.3 collective-permute-start.7
  119.8 1.3 collective-permute-start.6
  121.1 4.2 %collective-permute-start.5 = (f32[5,4,16,32]{3,2,1,0:T(8,128)S(1)}, f32[5,4,16,32]{3,2,1,0:T(8,128)S(1)}, u32[]{:S(2)}, u32[]{:S(2)}) collective-permute-start(f32[5,4,16,32]{3,2,1,0:T(8,128)S(1)} %copy.40), channel_id=1, source_target_pairs={{0,4},{4,8},{8,12},{12,16},{16,20},{20,24},{24,28},{1,5},{5,9},{9,... | collective-permute-start | bytes 122888 | tf_op jit(solution)/shard_map/ppermute | solution.py:26
  125.4 6.0 %collective-permute-done.5 = f32[5,4,16,32]{3,2,1,0:T(8,128)S(1)} collective-permute-done((f32[5,4,16,32]{3,2,1,0:T(8,128)S(1)}, f32[5,4,16,32]{3,2,1,0:T(8,128)S(1)}, u32[]{:S(2)}, u32[]{:S(2)}) %collective-permute-start.5) | collective-permute-done | bytes 40992 | tf_op jit(solution)/shard_map/ppermute | solution.py:26
  135.8 4.1 %collective-permute-start.8 = (f32[2,5,8,64]{3,2,1,0:T(8,128)S(1)}, f32[2,5,8,64]{3,2,1,0:T(8,128)S(1)}, u32[]{:S(2)}, u32[]{:S(2)}) collective-permute-start(f32[2,5,8,64]{3,2,1,0:T(8,128)S(1)} %get-tuple-element.135), channel_id=1, source_target_pairs={{0,4},{4,8},{8,12},{12,16},{16,20},{20,24},{24,28},{1,5},{5,9},{9,... | collective-permute-start | bytes 61448 | tf_op jit(solution)/shard_map/ppermute | solution.py:26
  140.0 1.3 collective-permute-start.9
  141.3 3.4 %collective-permute-done.9 = f32[2,5,8,64]{3,2,1,0:T(8,128)S(1)} collective-permute-done((f32[2,5,8,64]{3,2,1,0:T(8,128)S(1)}, f32[2,5,8,64]{3,2,1,0:T(8,128)S(1)}, u32[]{:S(2)}, u32[]{:S(2)}) %collective-permute-start.9) | collective-permute-done | bytes 20512 | tf_op jit(solution)/shard_map/ppermute | solution.py:26
  144.7 5.6 %collective-permute-start.10 = (f32[2,18,5,64]{3,2,1,0:T(8,128)S(1)}, f32[2,18,5,64]{3,2,1,0:T(8,128)S(1)}, u32[]{:S(2)}, u32[]{:S(2)}) collective-permute-start(f32[2,18,5,64]{3,2,1,0:T(8,128)S(1)} %get-tuple-element.91), channel_id=1, source_target_pairs={{0,1},{1,2},{2,3},{4,5},{5,6},{6,7},{8,9},{9,10},{10,11},{12,13},{... | collective-permute-start | bytes 138248 | tf_op jit(solution)/shard_map/ppermute | solution.py:26
  150.4 1.9 %collective-permute-start.11 = (f32[2,18,5,64]{3,2,1,0:T(8,128)S(1)}, f32[2,18,5,64]{3,2,1,0:T(8,128)S(1)}, u32[]{:S(2)}, u32[]{:S(2)}) collective-permute-start(f32[2,18,5,64]{3,2,1,0:T(8,128)S(1)} %get-tuple-element.92), channel_id=1, source_target_pairs={{1,0},{2,1},{3,2},{5,4},{6,5},{7,6},{9,8},{10,9},{11,10},{13,12},{... | collective-permute-start | bytes 138248 | tf_op jit(solution)/shard_map/ppermute | solution.py:26
  152.4 4.4 %collective-permute-done.11 = f32[2,18,5,64]{3,2,1,0:T(8,128)S(1)} collective-permute-done((f32[2,18,5,64]{3,2,1,0:T(8,128)S(1)}, f32[2,18,5,64]{3,2,1,0:T(8,128)S(1)}, u32[]{:S(2)}, u32[]{:S(2)}) %collective-permute-start.11) | collective-permute-done | bytes 46112 | tf_op jit(solution)/shard_map/ppermute | solution.py:26
  (168 shorter events, 29.7 us)
Async XLA Ops:
  0.0 8.6 %copy-start.8 = (f32[5,8]{1,0:T(8,128)S(1)}, f32[5,8]{1,0:T(8,128)}, u32[]{:S(2)}) copy-start(f32[5,8]{1,0:T(8,128)} %param.7) | copy-start | bytes 484
  2.1 20.2 %collective-permute-start = (f32[3,10,16,128]{3,1,2,0:T(8,128)S(1)}, f32[3,10,16,128]{3,1,2,0:T(8,128)S(1)}, u32[]{:S(2)}, u32[]{:S(2)}) collective-permute-start(f32[3,10,16,128]{3,1,2,0:T(8,128)S(1)} %get-tuple-element.62), channel_id=1, source_target_pairs={{0,4},{4,8},{8,12},{12,16},{16,20},{20,24},{24,28},{1,5},{5,9},{9,... | collective-permute-start | bytes 737288 | tf_op jit(solution)/shard_map/ppermute | solution.py:26
  6.1 16.2 %collective-permute-start.1 = (f32[3,10,16,128]{3,1,2,0:T(8,128)S(1)}, f32[3,10,16,128]{3,1,2,0:T(8,128)S(1)}, u32[]{:S(2)}, u32[]{:S(2)}) collective-permute-start(f32[3,10,16,128]{3,1,2,0:T(8,128)S(1)} %get-tuple-element.63), channel_id=1, source_target_pairs={{4,0},{8,4},{12,8},{16,12},{20,16},{24,20},{28,24},{5,1},{9,5},{13... | collective-permute-start | bytes 737288 | tf_op jit(solution)/shard_map/ppermute | solution.py:26
  7.4 76.7 %copy-start.9 = (s32[128]{0:T(128)}, s32[128]{0:T(128)S(1)}, u32[]{:S(2)}) copy-start(s32[128]{0:T(128)S(1)} %and_select_fusion.3) | copy-start | bytes 1540
  22.5 11.6 %collective-permute-start.2 = (f32[3,36,10,128]{3,1,2,0:T(8,128)S(1)}, f32[3,36,10,128]{3,1,2,0:T(8,128)S(1)}, u32[]{:S(2)}, u32[]{:S(2)}) collective-permute-start(f32[3,36,10,128]{3,1,2,0:T(8,128)S(1)} %get-tuple-element.37), channel_id=1, source_target_pairs={{0,1},{1,2},{2,3},{4,5},{5,6},{6,7},{8,9},{9,10},{10,11},{12,13},{... | collective-permute-start | bytes 1658888 | tf_op jit(solution)/shard_map/ppermute | solution.py:26
  27.1 11.5 %collective-permute-start.3 = (f32[3,36,10,128]{3,1,2,0:T(8,128)S(1)}, f32[3,36,10,128]{3,1,2,0:T(8,128)S(1)}, u32[]{:S(2)}, u32[]{:S(2)}) collective-permute-start(f32[3,36,10,128]{3,1,2,0:T(8,128)S(1)} %get-tuple-element.38), channel_id=1, source_target_pairs={{1,0},{2,1},{3,2},{5,4},{6,5},{7,6},{9,8},{10,9},{11,10},{13,12},{... | collective-permute-start | bytes 1658888 | tf_op jit(solution)/shard_map/ppermute | solution.py:26
  92.9 6.5 %copy-start = (f32[36,36,128]{2,0,1:T(8,128)}, f32[36,36,128]{2,0,1:T(8,128)S(1)}, u32[]{:S(2)}) copy-start(f32[36,36,128]{2,0,1:T(8,128)S(1)} %get-tuple-element.151) | copy-start | bytes 1990660
  94.1 2.1 %copy-start.5 = (f32[34,34,128]{2,0,1:T(8,128)}, f32[34,34,128]{2,0,1:T(8,128)S(1)}, u32[]{:S(2)}) copy-start(f32[34,34,128]{2,0,1:T(8,128)S(1)} %get-tuple-element.25) | copy-start | bytes 1775620
  103.1 4.0 %copy-start.12 = (s32[28]{0:T(128)S(1)}, s32[28]{0:T(128)}, u32[]{:S(2)}) copy-start(s32[28]{0:T(128)} %and_select_fusion.4) | copy-start | bytes 340
  103.1 4.4 %copy-start.2 = (f32[18,18,63]{2,1,0:T(8,128)S(1)}, f32[18,18,63]{2,1,0:T(8,128)}, u32[]{:S(2)}) copy-start(f32[18,18,63]{2,1,0:T(8,128)} %divide_multiply_fusion) | copy-start | bytes 244948
  103.1 4.4 %copy-start.3 = (f32[17,18,64]{2,1,0:T(8,128)S(1)}, f32[17,18,64]{2,1,0:T(8,128)}, u32[]{:S(2)}) copy-start(f32[17,18,64]{2,1,0:T(8,128)} %multiply_bitcast_fusion) | copy-start | bytes 235012
  103.1 4.4 %copy-start.4 = (f32[18,17,64]{2,1,0:T(8,128)S(1)}, f32[18,17,64]{2,1,0:T(8,128)}, u32[]{:S(2)}) copy-start(f32[18,17,64]{2,1,0:T(8,128)} %divide_multiply_fusion.1) | copy-start | bytes 235012
  103.1 4.4 %copy-start.7 = (f32[18,18,64]{2,1,0:T(8,128)S(1)}, f32[18,18,64]{2,1,0:T(8,128)}, u32[]{:S(2)}) copy-start(f32[18,18,64]{2,1,0:T(8,128)} %get-tuple-element.40) | copy-start | bytes 248836
  107.5 0.8 copy-start.11
  113.4 11.9 %collective-permute-start.4 = (f32[5,4,16,32]{3,2,1,0:T(8,128)S(1)}, f32[5,4,16,32]{3,2,1,0:T(8,128)S(1)}, u32[]{:S(2)}, u32[]{:S(2)}) collective-permute-start(f32[5,4,16,32]{3,2,1,0:T(8,128)S(1)} %copy.40), channel_id=1, source_target_pairs={{0,8},{4,12},{8,16},{12,20},{16,24},{20,28},{1,9},{5,13},{9,17},{1... | collective-permute-start | bytes 122888 | tf_op jit(solution)/shard_map/ppermute | solution.py:26
  118.5 13.0 %collective-permute-start.7 = (f32[5,4,16,32]{3,2,1,0:T(8,128)S(1)}, f32[5,4,16,32]{3,2,1,0:T(8,128)S(1)}, u32[]{:S(2)}, u32[]{:S(2)}) collective-permute-start(f32[5,4,16,32]{3,2,1,0:T(8,128)S(1)} %copy.40), channel_id=1, source_target_pairs={{8,0},{12,4},{16,8},{20,12},{24,16},{28,20},{9,1},{13,5},{17,9},{2... | collective-permute-start | bytes 122888 | tf_op jit(solution)/shard_map/ppermute | solution.py:26
  119.8 11.6 %collective-permute-start.6 = (f32[5,4,16,32]{3,2,1,0:T(8,128)S(1)}, f32[5,4,16,32]{3,2,1,0:T(8,128)S(1)}, u32[]{:S(2)}, u32[]{:S(2)}) collective-permute-start(f32[5,4,16,32]{3,2,1,0:T(8,128)S(1)} %copy.40), channel_id=1, source_target_pairs={{4,0},{8,4},{12,8},{16,12},{20,16},{24,20},{28,24},{5,1},{9,5},{13... | collective-permute-start | bytes 122888 | tf_op jit(solution)/shard_map/ppermute | solution.py:26
  121.1 10.3 %collective-permute-start.5 = (f32[5,4,16,32]{3,2,1,0:T(8,128)S(1)}, f32[5,4,16,32]{3,2,1,0:T(8,128)S(1)}, u32[]{:S(2)}, u32[]{:S(2)}) collective-permute-start(f32[5,4,16,32]{3,2,1,0:T(8,128)S(1)} %copy.40), channel_id=1, source_target_pairs={{0,4},{4,8},{8,12},{12,16},{16,20},{20,24},{24,28},{1,5},{5,9},{9,... | collective-permute-start | bytes 122888 | tf_op jit(solution)/shard_map/ppermute | solution.py:26
  135.8 5.4 %collective-permute-start.8 = (f32[2,5,8,64]{3,2,1,0:T(8,128)S(1)}, f32[2,5,8,64]{3,2,1,0:T(8,128)S(1)}, u32[]{:S(2)}, u32[]{:S(2)}) collective-permute-start(f32[2,5,8,64]{3,2,1,0:T(8,128)S(1)} %get-tuple-element.135), channel_id=1, source_target_pairs={{0,4},{4,8},{8,12},{12,16},{16,20},{20,24},{24,28},{1,5},{5,9},{9,... | collective-permute-start | bytes 61448 | tf_op jit(solution)/shard_map/ppermute | solution.py:26
  140.0 4.7 %collective-permute-start.9 = (f32[2,5,8,64]{3,2,1,0:T(8,128)S(1)}, f32[2,5,8,64]{3,2,1,0:T(8,128)S(1)}, u32[]{:S(2)}, u32[]{:S(2)}) collective-permute-start(f32[2,5,8,64]{3,2,1,0:T(8,128)S(1)} %get-tuple-element.136), channel_id=1, source_target_pairs={{4,0},{8,4},{12,8},{16,12},{20,16},{24,20},{28,24},{5,1},{9,5},{13... | collective-permute-start | bytes 61448 | tf_op jit(solution)/shard_map/ppermute | solution.py:26
  144.7 7.7 %collective-permute-start.10 = (f32[2,18,5,64]{3,2,1,0:T(8,128)S(1)}, f32[2,18,5,64]{3,2,1,0:T(8,128)S(1)}, u32[]{:S(2)}, u32[]{:S(2)}) collective-permute-start(f32[2,18,5,64]{3,2,1,0:T(8,128)S(1)} %get-tuple-element.91), channel_id=1, source_target_pairs={{0,1},{1,2},{2,3},{4,5},{5,6},{6,7},{8,9},{9,10},{10,11},{12,13},{... | collective-permute-start | bytes 138248 | tf_op jit(solution)/shard_map/ppermute | solution.py:26
  150.4 6.5 %collective-permute-start.11 = (f32[2,18,5,64]{3,2,1,0:T(8,128)S(1)}, f32[2,18,5,64]{3,2,1,0:T(8,128)S(1)}, u32[]{:S(2)}, u32[]{:S(2)}) collective-permute-start(f32[2,18,5,64]{3,2,1,0:T(8,128)S(1)} %get-tuple-element.92), channel_id=1, source_target_pairs={{1,0},{2,1},{3,2},{5,4},{6,5},{7,6},{9,8},{10,9},{11,10},{13,12},{... | collective-permute-start | bytes 138248 | tf_op jit(solution)/shard_map/ppermute | solution.py:26
  157.5 0.7 copy-start.10
  158.6 1.1 copy-start.1
  158.6 1.3 copy-start.6
where the time goes:
time: 163 us; the launch traced here: 162 us
  other arithmetic  64.4 us (40%)
  starting transfers between devices  36.6 us (22%)
  waiting for transfers between devices  35 us (21%)
  local copies, waits for them, and re-layouts  16.8 us (10%)
  blocking collectives  4.37 us (3%)
  matrix products  4.22 us (3%)
    ppermute x12, starting transfers between devices, shift_from(): return lax.ppermute(cells, axis, pairs)  36.6 us
    ppermute x12, waiting for transfers between devices, shift_from(): return lax.ppermute(cells, axis, pairs)  35 us
    select_n x2, other arithmetic, local(): kx = jnp.where(inside, lookup(ids, soil_table, 0), 0.0)  11.7 us
    select_n x2, other arithmetic, local(): kz = jnp.where(inside, lookup(ids, soil_table, 2), 0.0)  11.4 us
    select_n x1, other arithmetic, local(): store = jnp.where(inside, store, 0.0)  11 us
    select_n x2, other arithmetic, local(): ky = jnp.where(inside, lookup(ids, soil_table, 1), 0.0)  11 us
    all_gather x1, blocking collectives, local(): cpack = lax.all_gather(cpack, 'gy', axis=2, tiled=True)  4.37 us
    add x7, other arithmetic, chebyshev(): iterate = win(iterate, n, cur, nxt) + update  3.87 us
  transfers between devices with their start and end apart: 12, of which 7 were waited for; matrix products, arithmetic and copies ran while one was open for 2% of the time, Pallas kernels for 0%

commit v1 on v0

--- a/solution.py
+++ b/solution.py
@@ -192,7 +192,12 @@
     nc = b2.shape[0]
     reach = 2
     cpack = jnp.concatenate([b2[None], coarse_own], axis=0)
-    cpack = lax.all_gather(cpack, "gy", axis=2, tiled=True)
+    ring = [cpack]
+    for hop in range(3):
+        ring.append(lax.ppermute(ring[-1], "gy", [(dev, (dev + 1) % 4) for dev in range(4)]))
+    cpack = jnp.roll(
+        jnp.concatenate(ring[::-1], axis=2), (lax.axis_index("gy") + 1) * ring[0].shape[2], axis=2
+    )
     parts = [shift_from(cpack, "gx", -d) for d in range(reach, 0, -1)]
     parts += [cpack]
     parts += [shift_from(cpack, "gx", d) for d in range(1, reach + 1)]

time: 163 us -> 179 us (1.098); the launches traced: 162 us -> 176 us
  local copies, waits for them, and re-layouts: 16.8 us -> 27.4 us
  blocking collectives: 4.37 us -> 0 us
  waiting for transfers between devices: 35 us -> 38.8 us
  starting transfers between devices: 36.6 us -> 39.5 us
    concatenate x1, local copies, waits for them, and re-layouts: 0.01 us -> 5.9 us  [local(): jnp.roll(jnp.concatenate(ring[::-1], axis=2), (lax.axis_index('gy') + 1)...]
    ppermute x0 -> x3, starting transfers between devices: none -> 4.64 us  [local(): lax.ppermute(ring[-1], 'gy', [(dev, (dev + 1) % 4) for dev in range(4)])]
    all_gather x1 -> x0, blocking collectives: 4.37 us -> none  [local(): cpack = lax.all_gather(cpack, 'gy', axis=2, tiled=True)]
    ppermute x0 -> x3, waiting for transfers between devices: none -> 3.73 us  [local(): lax.ppermute(ring[-1], 'gy', [(dev, (dev + 1) % 4) for dev in range(4)])]
    unnamed x29 -> x50, local copies, waits for them, and re-layouts: 0.66 us -> 2.96 us
  transfers between devices with their start and end apart: 12 -> 15, of which waited for: 7 -> 10; matrix products, arithmetic and copies ran while one was open for 2% -> 3% of each run, Pallas kernels for 0% -> 0%
where the time goes in v1:
time: 179 us; the launch traced here: 176 us
  other arithmetic  65.7 us (37%)
  starting transfers between devices  39.5 us (22%)
  waiting for transfers between devices  38.8 us (22%)
  local copies, waits for them, and re-layouts  27.4 us (15%)
  matrix products  3.56 us (2%)
    ppermute x12, waiting for transfers between devices, shift_from(): return lax.ppermute(cells, axis, pairs)  35.1 us
    ppermute x12, starting transfers between devices, shift_from(): return lax.ppermute(cells, axis, pairs)  34.9 us
    select_n x2, other arithmetic, local(): kx = jnp.where(inside, lookup(ids, soil_table, 0), 0.0)  11.7 us
    select_n x2, other arithmetic, local(): ky = jnp.where(inside, lookup(ids, soil_table, 1), 0.0)  11.2 us
    select_n x1, other arithmetic, local(): store = jnp.where(inside, store, 0.0)  11.2 us
    select_n x2, other arithmetic, local(): kz = jnp.where(inside, lookup(ids, soil_table, 2), 0.0)  10.9 us
    concatenate x1, local copies, waits for them, and re-layouts, local(): jnp.roll(jnp.concatenate(ring[::-1], axis=2), (lax.axis_index('gy') + 1)...  5.9 us
    ppermute x3, starting transfers between devices, local(): lax.ppermute(ring[-1], 'gy', [(dev, (dev + 1) % 4) for dev in range(4)])  4.64 us
  transfers between devices with their start and end apart: 15, of which 10 were waited for; matrix products, arithmetic and copies ran while one was open for 3% of the time, Pallas kernels for 0%

profile of v1, /device:TPU:1, one launch (start us, length us, event | category | flops | bytes accessed | tf_op | source)
XLA Modules:
  0.0 176.1 jit_solution(12937632107012172874)
XLA Ops:
  2.1 4.0 %collective-permute-start = (f32[3,10,16,128]{3,1,2,0:T(8,128)S(1)}, f32[3,10,16,128]{3,1,2,0:T(8,128)S(1)}, u32[]{:S(2)}, u32[]{:S(2)}) collective-permute-start(f32[3,10,16,128]{3,1,2,0:T(8,128)S(1)} %get-tuple-element.62), channel_id=1, source_target_pairs={{0,4},{4,8},{8,12},{12,16},{16,20},{20,24},{24,28},{1,5},{5,9},{9,... | collective-permute-start | bytes 737288 | tf_op jit(solution)/shard_map/ppermute | solution.py:26
  6.1 1.3 collective-permute-start.1
  9.2 13.1 %collective-permute-done = f32[3,10,16,128]{3,1,2,0:T(8,128)S(1)} collective-permute-done((f32[3,10,16,128]{3,1,2,0:T(8,128)S(1)}, f32[3,10,16,128]{3,1,2,0:T(8,128)S(1)}, u32[]{:S(2)}, u32[]{:S(2)}) %collective-permute-start) | collective-permute-done | bytes 245792 | tf_op jit(solution)/shard_map/ppermute | solution.py:26
  22.5 4.6 %collective-permute-start.2 = (f32[3,36,10,128]{3,1,2,0:T(8,128)S(1)}, f32[3,36,10,128]{3,1,2,0:T(8,128)S(1)}, u32[]{:S(2)}, u32[]{:S(2)}) collective-permute-start(f32[3,36,10,128]{3,1,2,0:T(8,128)S(1)} %get-tuple-element.37), channel_id=1, source_target_pairs={{0,1},{1,2},{2,3},{4,5},{5,6},{6,7},{8,9},{9,10},{10,11},{12,13},{... | collective-permute-start | bytes 1658888 | tf_op jit(solution)/shard_map/ppermute | solution.py:26
  27.1 1.9 %collective-permute-start.3 = (f32[3,36,10,128]{3,1,2,0:T(8,128)S(1)}, f32[3,36,10,128]{3,1,2,0:T(8,128)S(1)}, u32[]{:S(2)}, u32[]{:S(2)}) collective-permute-start(f32[3,36,10,128]{3,1,2,0:T(8,128)S(1)} %get-tuple-element.38), channel_id=1, source_target_pairs={{1,0},{2,1},{3,2},{5,4},{6,5},{7,6},{9,8},{10,9},{11,10},{13,12},{... | collective-permute-start | bytes 1658888 | tf_op jit(solution)/shard_map/ppermute | solution.py:26
  30.6 3.6 %collective-permute-done.2 = f32[3,36,10,128]{3,1,2,0:T(8,128)S(1)} collective-permute-done((f32[3,36,10,128]{3,1,2,0:T(8,128)S(1)}, f32[3,36,10,128]{3,1,2,0:T(8,128)S(1)}, u32[]{:S(2)}, u32[]{:S(2)}) %collective-permute-start.2) | collective-permute-done | bytes 552992 | tf_op jit(solution)/shard_map/ppermute | solution.py:26
  34.1 4.4 %collective-permute-done.3 = f32[3,36,10,128]{3,1,2,0:T(8,128)S(1)} collective-permute-done((f32[3,36,10,128]{3,1,2,0:T(8,128)S(1)}, f32[3,36,10,128]{3,1,2,0:T(8,128)S(1)}, u32[]{:S(2)}, u32[]{:S(2)}) %collective-permute-start.3) | collective-permute-done | bytes 552992 | tf_op jit(solution)/shard_map/ppermute | solution.py:26
  38.7 6.1 %broadcast_select_fusion.3 = (f32[1,36,36,128]{3,1,2,0:T(8,128)S(1)}, pred[1,36,36,128]{3,1,2,0:T(8,128)(4,1)S(1)}, pred[1,36,36,128]{3,1,2,0:T(8,128)(4,1)S(1)}...) fusion(pred[36,36]{0,1:T(8,128)(4,1)S(1)} %broadcast_and_fusion, ...), kind=kLoop, calls=%fused_computation.137 | loop fusion | flops 2654208 | bytes 3816752 | tf_op jit(solution)/shard_map/jit(_where)/select_n | solution.py:169
  44.8 5.6 %broadcast_select_fusion.2 = f32[1,36,36,128]{3,1,2,0:T(8,128)S(1)} fusion(pred[36,36]{0,1:T(8,128)(4,1)S(1)} %broadcast_and_fusion, pred[1,36,36,128]{3,1,2,0:T(8,128)(4,1)S(1)} %get-tuple-element.33, pred[1,36,36,128]{3,1,2,0:T(8,128)(4,1)S(1)} %get-tuple-element.32, pred[1,36,36,128]{3,1,2,0:T(8,128)(4,1)S(1)} %get-tuple-element.31, ...), kind=kLoop, calls=%fused_computation.136 | loop fusion | flops 1327104 | bytes 1826096 | tf_op jit(solution)/shard_map/jit(_where)/select_n | solution.py:170
  50.5 5.6 %bitcast_select_fusion.2 = f32[36,36,128]{2,0,1:T(8,128)S(1)} fusion(pred[36,36]{0,1:T(8,128)(4,1)S(1)} %broadcast_and_fusion, pred[1,36,36,128]{3,1,2,0:T(8,128)(4,1)S(1)} %get-tuple-element.33, pred[1,36,36,128]{3,1,2,0:T(8,128)(4,1)S(1)} %get-tuple-element.32, pred[1,36,36,128]{3,1,2,0:T(8,128)(4,1)S(1)} %get-tuple-element.31, ...), kind=kLoop, calls=%fused_computation.31 | loop fusion | flops 1327104 | bytes 1826096 | tf_op jit(solution)/shard_map/jit(_where)/select_n | solution.py:170
  56.1 5.4 %broadcast_select_fusion.1 = f32[1,36,36,128]{3,1,2,0:T(8,128)S(1)} fusion(pred[36,36]{0,1:T(8,128)(4,1)S(1)} %broadcast_and_fusion, pred[1,36,36,128]{3,1,2,0:T(8,128)(4,1)S(1)} %get-tuple-element.33, pred[1,36,36,128]{3,1,2,0:T(8,128)(4,1)S(1)} %get-tuple-element.32, pred[1,36,36,128]{3,1,2,0:T(8,128)(4,1)S(1)} %get-tuple-element.31, ...), kind=kLoop, calls=%fused_computation.135 | loop fusion | flops 1327104 | bytes 1826096 | tf_op jit(solution)/shard_map/jit(_where)/select_n | solution.py:171
  61.6 5.4 %bitcast_select_fusion.1 = f32[36,36,128]{2,0,1:T(8,128)S(1)} fusion(pred[36,36]{0,1:T(8,128)(4,1)S(1)} %broadcast_and_fusion, pred[1,36,36,128]{3,1,2,0:T(8,128)(4,1)S(1)} %get-tuple-element.33, pred[1,36,36,128]{3,1,2,0:T(8,128)(4,1)S(1)} %get-tuple-element.32, pred[1,36,36,128]{3,1,2,0:T(8,128)(4,1)S(1)} %get-tuple-element.31, ...), kind=kLoop, calls=%fused_computation.30 | loop fusion | flops 1327104 | bytes 1826096 | tf_op jit(solution)/shard_map/jit(_where)/select_n | solution.py:171
  67.7 11.2 %broadcast_select_fusion = (f32[1,36,36,128]{3,1,2,0:T(8,128)S(1)}, f32[1,36,36,128]{3,1,2,0:T(8,128)S(1)}) fusion(pred[36,36]{0,1:T(8,128)(4,1)S(1)} %broadcast_and_fusion, f32[3,36,36,128]{3,1,2,0:T(8,128)S(1)} %pad_maximum_fusion.1, pred[1,36,36,128]{3,1,2,0:T(8,128)(4,1)S(1)} %get-tuple-element.33, pred[1,36,36,128]{3,1,2,0:T(8,128)(4,1)S(1)} %get-tuple-element.32, ...), kind=kLoop, calls=%fused_computation.134 | loop fusion | flops 3317760 | bytes 3153232 | tf_op jit(solution)/shard_map/jit(_where)/select_n | solution.py:175
  81.0 2.7 %pad_maximum_fusion = f32[4,18,2,36,128]{4,0,3,2,1:T(4,128)S(1)} fusion(f32[1,18,2,36,128]{4,0,3,2,1:T(1,128)S(1)} %bitcast.252, f32[1,18,2,36,128]{4,0,3,2,1:T(1,128)S(1)} %bitcast.254, f32[1,18,2,36,128]{4,0,3,2,1:T(1,128)S(1)} %bitcast.253, f32[1,18,2,36,128]{4,0,3,2,1:T(1,128)S(1)} %bitcast.251), kind=kLoop, calls=%fused_computation | loop fusion | flops 1990656 | bytes 5308416 | tf_op jit(solution)/shard_map/stack | solution.py:176
  87.9 5.6 %bitcast_select_fusion.3 = (f32[36,36,128]{2,0,1:T(8,128)S(1)}, f32[36,36,128]{2,0,1:T(8,128)S(1)}) fusion(pred[36,36]{0,1:T(8,128)(4,1)S(1)} %broadcast_and_fusion, pred[1,36,36,128]{3,1,2,0:T(8,128)(4,1)S(1)} %get-tuple-element.33, pred[1,36,36,128]{3,1,2,0:T(8,128)(4,1)S(1)} %get-tuple-element.32, pred[1,36,36,128]{3,1,2,0:T(8,128)(4,1)S(1)} %get-tuple-element.31, ...), kind=kLoop, calls=%fused_computation.32 | loop fusion | flops 1492992 | bytes 3153200 | tf_op jit(solution)/shard_map/jit(_where)/select_n | solution.py:169
  100.0 1.7 fusion.58
  101.7 2.0 %reshape.377 = f32[14,2,28,128]{3,1,0,2:T(2,128)} reshape(f32[28,28,128]{2,0,1:T(8,128)} %fusion.58) | data formatting | bytes 802816 | tf_op jit(solution)/shard_map/reshape | solution.py:59
  103.7 1.5 fusion.427
  105.6 1.5 add_maximum_fusion.1
  112.1 2.2 %collective-permute-start.5 = (f32[5,4,4,32]{3,2,1,0:T(4,128)S(1)}, f32[5,4,4,32]{3,2,1,0:T(4,128)}, u32[]{:S(2)}, u32[]{:S(2)}) collective-permute-start(f32[5,4,4,32]{3,2,1,0:T(4,128)S(1)} %collective-permute-done.4), channel_id=1, source_target_pairs={{0,1},{1,2},{2,3},{3,0},{4,5},{5,6},{6,7},{7,4},{8,9},{9,10},{10,1... | collective-permute-start | bytes 30728 | tf_op jit(solution)/shard_map/ppermute | solution.py:197
  115.5 2.4 %collective-permute-start.6 = (f32[5,4,4,32]{3,2,1,0:T(4,128)}, f32[5,4,4,32]{3,2,1,0:T(4,128)}, u32[]{:S(2)}, u32[]{:S(2)}) collective-permute-start(f32[5,4,4,32]{3,2,1,0:T(4,128)} %collective-permute-done.5), channel_id=1, source_target_pairs={{0,1},{1,2},{2,3},{3,0},{4,5},{5,6},{6,7},{7,4},{8,9},{9,10},{10,1... | collective-permute-start | bytes 30728 | tf_op jit(solution)/shard_map/ppermute | solution.py:197
  117.9 1.4 collective-permute-done.6
  119.3 5.9 %concatenate.188 = f32[5,4,32,32]{3,2,1,0:T(8,128)} concatenate(f32[5,4,4,32]{3,2,1,0:T(4,128)} %collective-permute-done.6, f32[5,4,4,32]{3,2,1,0:T(4,128)} %collective-permute-done.5, f32[5,4,4,32]{3,2,1,0:T(4,128)} %copy-done.16, f32[5,4,4,32]{3,2,1,0:T(4,128)} %copy-done.14, f32[5,4,4,32]{3,2,1,0:T(4,128)} %collective-permute-done.6, f32[5,4,4,32]{3,2,1,0:T(4,128)} %collective-permute-done.5, ...), dimensions={2} | concatenate | bytes 163840 | tf_op jit(solution)/shard_map/jit(_roll_dynamic)/concatenate | solution.py:198
  126.2 5.1 %collective-permute-start.7 = (f32[5,4,16,32]{3,2,1,0:T(8,128)S(1)}, f32[5,4,16,32]{3,2,1,0:T(8,128)S(1)}, u32[]{:S(2)}, u32[]{:S(2)}) collective-permute-start(f32[5,4,16,32]{3,2,1,0:T(8,128)S(1)} %constant_dynamic-slice_fusion), channel_id=1, source_target_pairs={{0,8},{4,12},{8,16},{12,20},{16,24},{20,28},{1,9},{5,13},{9,17},{1... | collective-permute-start | bytes 122888 | tf_op jit(solution)/shard_map/ppermute | solution.py:26
  134.7 4.2 %collective-permute-start.8 = (f32[5,4,16,32]{3,2,1,0:T(8,128)S(1)}, f32[5,4,16,32]{3,2,1,0:T(8,128)S(1)}, u32[]{:S(2)}, u32[]{:S(2)}) collective-permute-start(f32[5,4,16,32]{3,2,1,0:T(8,128)S(1)} %constant_dynamic-slice_fusion), channel_id=1, source_target_pairs={{0,4},{4,8},{8,12},{12,16},{16,20},{20,24},{24,28},{1,5},{5,9},{9,... | collective-permute-start | bytes 122888 | tf_op jit(solution)/shard_map/ppermute | solution.py:26
  138.9 6.1 %collective-permute-done.8 = f32[5,4,16,32]{3,2,1,0:T(8,128)S(1)} collective-permute-done((f32[5,4,16,32]{3,2,1,0:T(8,128)S(1)}, f32[5,4,16,32]{3,2,1,0:T(8,128)S(1)}, u32[]{:S(2)}, u32[]{:S(2)}) %collective-permute-start.8) | collective-permute-done | bytes 40992 | tf_op jit(solution)/shard_map/ppermute | solution.py:26
  151.2 4.1 %collective-permute-start.11 = (f32[2,5,8,64]{3,2,1,0:T(8,128)S(1)}, f32[2,5,8,64]{3,2,1,0:T(8,128)S(1)}, u32[]{:S(2)}, u32[]{:S(2)}) collective-permute-start(f32[2,5,8,64]{3,2,1,0:T(8,128)S(1)} %get-tuple-element.129), channel_id=1, source_target_pairs={{0,4},{4,8},{8,12},{12,16},{16,20},{20,24},{24,28},{1,5},{5,9},{9,... | collective-permute-start | bytes 61448 | tf_op jit(solution)/shard_map/ppermute | solution.py:26
  155.3 1.3 collective-permute-start.12
  156.7 3.4 %collective-permute-done.12 = f32[2,5,8,64]{3,2,1,0:T(8,128)S(1)} collective-permute-done((f32[2,5,8,64]{3,2,1,0:T(8,128)S(1)}, f32[2,5,8,64]{3,2,1,0:T(8,128)S(1)}, u32[]{:S(2)}, u32[]{:S(2)}) %collective-permute-start.12) | collective-permute-done | bytes 20512 | tf_op jit(solution)/shard_map/ppermute | solution.py:26
  160.1 3.9 %collective-permute-start.13 = (f32[2,18,5,64]{3,2,1,0:T(8,128)S(1)}, f32[2,18,5,64]{3,2,1,0:T(8,128)S(1)}, u32[]{:S(2)}, u32[]{:S(2)}) collective-permute-start(f32[2,18,5,64]{3,2,1,0:T(8,128)S(1)} %get-tuple-element.85), channel_id=1, source_target_pairs={{0,1},{1,2},{2,3},{4,5},{5,6},{6,7},{8,9},{9,10},{10,11},{12,13},{... | collective-permute-start | bytes 138248 | tf_op jit(solution)/shard_map/ppermute | solution.py:26
  164.1 1.9 %collective-permute-start.14 = (f32[2,18,5,64]{3,2,1,0:T(8,128)S(1)}, f32[2,18,5,64]{3,2,1,0:T(8,128)S(1)}, u32[]{:S(2)}, u32[]{:S(2)}) collective-permute-start(f32[2,18,5,64]{3,2,1,0:T(8,128)S(1)} %get-tuple-element.86), channel_id=1, source_target_pairs={{1,0},{2,1},{3,2},{5,4},{6,5},{7,6},{9,8},{10,9},{11,10},{13,12},{... | collective-permute-start | bytes 138248 | tf_op jit(solution)/shard_map/ppermute | solution.py:26
  166.2 4.4 %collective-permute-done.14 = f32[2,18,5,64]{3,2,1,0:T(8,128)S(1)} collective-permute-done((f32[2,18,5,64]{3,2,1,0:T(8,128)S(1)}, f32[2,18,5,64]{3,2,1,0:T(8,128)S(1)}, u32[]{:S(2)}, u32[]{:S(2)}) %collective-permute-start.14) | collective-permute-done | bytes 46112 | tf_op jit(solution)/shard_map/ppermute | solution.py:26
  (193 shorter events, 41.2 us)
Async XLA Ops:
  0.0 8.6 %copy-start.17 = (f32[5,8]{1,0:T(8,128)S(1)}, f32[5,8]{1,0:T(8,128)}, u32[]{:S(2)}) copy-start(f32[5,8]{1,0:T(8,128)} %param.7) | copy-start | bytes 484
  2.1 20.2 %collective-permute-start = (f32[3,10,16,128]{3,1,2,0:T(8,128)S(1)}, f32[3,10,16,128]{3,1,2,0:T(8,128)S(1)}, u32[]{:S(2)}, u32[]{:S(2)}) collective-permute-start(f32[3,10,16,128]{3,1,2,0:T(8,128)S(1)} %get-tuple-element.62), channel_id=1, source_target_pairs={{0,4},{4,8},{8,12},{12,16},{16,20},{20,24},{24,28},{1,5},{5,9},{9,... | collective-permute-start | bytes 737288 | tf_op jit(solution)/shard_map/ppermute | solution.py:26
  6.1 16.2 %collective-permute-start.1 = (f32[3,10,16,128]{3,1,2,0:T(8,128)S(1)}, f32[3,10,16,128]{3,1,2,0:T(8,128)S(1)}, u32[]{:S(2)}, u32[]{:S(2)}) collective-permute-start(f32[3,10,16,128]{3,1,2,0:T(8,128)S(1)} %get-tuple-element.63), channel_id=1, source_target_pairs={{4,0},{8,4},{12,8},{16,12},{20,16},{24,20},{28,24},{5,1},{9,5},{13... | collective-permute-start | bytes 737288 | tf_op jit(solution)/shard_map/ppermute | solution.py:26
  7.4 97.9 %copy-start.18 = (s32[128]{0:T(128)}, s32[128]{0:T(128)S(1)}, u32[]{:S(2)}) copy-start(s32[128]{0:T(128)S(1)} %and_select_fusion.3) | copy-start | bytes 1540
  22.5 11.6 %collective-permute-start.2 = (f32[3,36,10,128]{3,1,2,0:T(8,128)S(1)}, f32[3,36,10,128]{3,1,2,0:T(8,128)S(1)}, u32[]{:S(2)}, u32[]{:S(2)}) collective-permute-start(f32[3,36,10,128]{3,1,2,0:T(8,128)S(1)} %get-tuple-element.37), channel_id=1, source_target_pairs={{0,1},{1,2},{2,3},{4,5},{5,6},{6,7},{8,9},{9,10},{10,11},{12,13},{... | collective-permute-start | bytes 1658888 | tf_op jit(solution)/shard_map/ppermute | solution.py:26
  27.1 11.5 %collective-permute-start.3 = (f32[3,36,10,128]{3,1,2,0:T(8,128)S(1)}, f32[3,36,10,128]{3,1,2,0:T(8,128)S(1)}, u32[]{:S(2)}, u32[]{:S(2)}) collective-permute-start(f32[3,36,10,128]{3,1,2,0:T(8,128)S(1)} %get-tuple-element.38), channel_id=1, source_target_pairs={{1,0},{2,1},{3,2},{5,4},{6,5},{7,6},{9,8},{10,9},{11,10},{13,12},{... | collective-permute-start | bytes 1658888 | tf_op jit(solution)/shard_map/ppermute | solution.py:26
  93.5 6.5 %copy-start = (f32[36,36,128]{2,0,1:T(8,128)}, f32[36,36,128]{2,0,1:T(8,128)S(1)}, u32[]{:S(2)}) copy-start(f32[36,36,128]{2,0,1:T(8,128)S(1)} %get-tuple-element.145) | copy-start | bytes 1990660
  94.8 2.1 %copy-start.8 = (f32[34,34,128]{2,0,1:T(8,128)}, f32[34,34,128]{2,0,1:T(8,128)S(1)}, u32[]{:S(2)}) copy-start(f32[34,34,128]{2,0,1:T(8,128)S(1)} %get-tuple-element.25) | copy-start | bytes 1775620
  103.7 3.3 %copy-start.22 = (s32[28]{0:T(128)S(1)}, s32[28]{0:T(128)}, u32[]{:S(2)}) copy-start(s32[28]{0:T(128)} %and_select_fusion.4) | copy-start | bytes 340
  103.7 3.7 %copy-start.2 = (f32[18,18,63]{2,1,0:T(8,128)S(1)}, f32[18,18,63]{2,1,0:T(8,128)}, u32[]{:S(2)}) copy-start(f32[18,18,63]{2,1,0:T(8,128)} %divide_multiply_fusion) | copy-start | bytes 244948
  103.7 3.8 %copy-start.4 = (f32[17,18,64]{2,1,0:T(8,128)S(1)}, f32[17,18,64]{2,1,0:T(8,128)}, u32[]{:S(2)}) copy-start(f32[17,18,64]{2,1,0:T(8,128)} %multiply_bitcast_fusion) | copy-start | bytes 235012
  103.7 3.8 %copy-start.6 = (f32[18,17,64]{2,1,0:T(8,128)S(1)}, f32[18,17,64]{2,1,0:T(8,128)}, u32[]{:S(2)}) copy-start(f32[18,17,64]{2,1,0:T(8,128)} %divide_multiply_fusion.1) | copy-start | bytes 235012
  103.7 3.8 %copy-start.10 = (f32[18,18,64]{2,1,0:T(8,128)S(1)}, f32[18,18,64]{2,1,0:T(8,128)}, u32[]{:S(2)}) copy-start(f32[18,18,64]{2,1,0:T(8,128)} %get-tuple-element.40) | copy-start | bytes 248836
  108.2 1.1 copy-start.12
  110.3 1.2 collective-permute-start.4
  112.1 3.3 %collective-permute-start.5 = (f32[5,4,4,32]{3,2,1,0:T(4,128)S(1)}, f32[5,4,4,32]{3,2,1,0:T(4,128)}, u32[]{:S(2)}, u32[]{:S(2)}) collective-permute-start(f32[5,4,4,32]{3,2,1,0:T(4,128)S(1)} %collective-permute-done.4), channel_id=1, source_target_pairs={{0,1},{1,2},{2,3},{3,0},{4,5},{5,6},{6,7},{7,4},{8,9},{9,10},{10,1... | collective-permute-start | bytes 30728 | tf_op jit(solution)/shard_map/ppermute | solution.py:197
  115.5 3.8 %collective-permute-start.6 = (f32[5,4,4,32]{3,2,1,0:T(4,128)}, f32[5,4,4,32]{3,2,1,0:T(4,128)}, u32[]{:S(2)}, u32[]{:S(2)}) collective-permute-start(f32[5,4,4,32]{3,2,1,0:T(4,128)} %collective-permute-done.5), channel_id=1, source_target_pairs={{0,1},{1,2},{2,3},{3,0},{4,5},{5,6},{6,7},{7,4},{8,9},{9,10},{10,1... | collective-permute-start | bytes 30728 | tf_op jit(solution)/shard_map/ppermute | solution.py:197
  126.2 12.7 %collective-permute-start.7 = (f32[5,4,16,32]{3,2,1,0:T(8,128)S(1)}, f32[5,4,16,32]{3,2,1,0:T(8,128)S(1)}, u32[]{:S(2)}, u32[]{:S(2)}) collective-permute-start(f32[5,4,16,32]{3,2,1,0:T(8,128)S(1)} %constant_dynamic-slice_fusion), channel_id=1, source_target_pairs={{0,8},{4,12},{8,16},{12,20},{16,24},{20,28},{1,9},{5,13},{9,17},{1... | collective-permute-start | bytes 122888 | tf_op jit(solution)/shard_map/ppermute | solution.py:26
  132.1 14.0 %collective-permute-start.10 = (f32[5,4,16,32]{3,2,1,0:T(8,128)S(1)}, f32[5,4,16,32]{3,2,1,0:T(8,128)S(1)}, u32[]{:S(2)}, u32[]{:S(2)}) collective-permute-start(f32[5,4,16,32]{3,2,1,0:T(8,128)S(1)} %constant_dynamic-slice_fusion), channel_id=1, source_target_pairs={{8,0},{12,4},{16,8},{20,12},{24,16},{28,20},{9,1},{13,5},{17,9},{2... | collective-permute-start | bytes 122888 | tf_op jit(solution)/shard_map/ppermute | solution.py:26
  133.4 12.6 %collective-permute-start.9 = (f32[5,4,16,32]{3,2,1,0:T(8,128)S(1)}, f32[5,4,16,32]{3,2,1,0:T(8,128)S(1)}, u32[]{:S(2)}, u32[]{:S(2)}) collective-permute-start(f32[5,4,16,32]{3,2,1,0:T(8,128)S(1)} %constant_dynamic-slice_fusion), channel_id=1, source_target_pairs={{4,0},{8,4},{12,8},{16,12},{20,16},{24,20},{28,24},{5,1},{9,5},{13... | collective-permute-start | bytes 122888 | tf_op jit(solution)/shard_map/ppermute | solution.py:26
  134.7 10.3 %collective-permute-start.8 = (f32[5,4,16,32]{3,2,1,0:T(8,128)S(1)}, f32[5,4,16,32]{3,2,1,0:T(8,128)S(1)}, u32[]{:S(2)}, u32[]{:S(2)}) collective-permute-start(f32[5,4,16,32]{3,2,1,0:T(8,128)S(1)} %constant_dynamic-slice_fusion), channel_id=1, source_target_pairs={{0,4},{4,8},{8,12},{12,16},{16,20},{20,24},{24,28},{1,5},{5,9},{9,... | collective-permute-start | bytes 122888 | tf_op jit(solution)/shard_map/ppermute | solution.py:26
  149.3 2.0 %copy-start.13 = (f32[1,8,8,64]{3,2,1,0:T(8,128)S(1)}, f32[1,8,8,64]{3,2,1,0:T(8,128)}, u32[]{:S(2)}) copy-start(f32[1,8,8,64]{3,2,1,0:T(8,128)} %get-tuple-element.108) | copy-start | bytes 49156
  149.8 21.0 %copy-start.3 = (f32[18,18,63]{2,1,0:T(8,128)S(1)}, f32[18,18,63]{2,1,0:T(8,128)}, u32[]{:S(2)}) copy-start(f32[18,18,63]{2,1,0:T(8,128)} %divide_multiply_fusion) | copy-start | bytes 244948
  149.8 21.1 %copy-start.5 = (f32[17,18,64]{2,1,0:T(8,128)S(1)}, f32[17,18,64]{2,1,0:T(8,128)}, u32[]{:S(2)}) copy-start(f32[17,18,64]{2,1,0:T(8,128)} %multiply_bitcast_fusion) | copy-start | bytes 235012
  149.9 21.1 %copy-start.7 = (f32[18,17,64]{2,1,0:T(8,128)S(1)}, f32[18,17,64]{2,1,0:T(8,128)}, u32[]{:S(2)}) copy-start(f32[18,17,64]{2,1,0:T(8,128)} %divide_multiply_fusion.1) | copy-start | bytes 235012
  149.9 21.1 %copy-start.11 = (f32[18,18,64]{2,1,0:T(8,128)S(1)}, f32[18,18,64]{2,1,0:T(8,128)}, u32[]{:S(2)}) copy-start(f32[18,18,64]{2,1,0:T(8,128)} %get-tuple-element.40) | copy-start | bytes 248836
  151.2 5.4 %collective-permute-start.11 = (f32[2,5,8,64]{3,2,1,0:T(8,128)S(1)}, f32[2,5,8,64]{3,2,1,0:T(8,128)S(1)}, u32[]{:S(2)}, u32[]{:S(2)}) collective-permute-start(f32[2,5,8,64]{3,2,1,0:T(8,128)S(1)} %get-tuple-element.129), channel_id=1, source_target_pairs={{0,4},{4,8},{8,12},{12,16},{16,20},{20,24},{24,28},{1,5},{5,9},{9,... | collective-permute-start | bytes 61448 | tf_op jit(solution)/shard_map/ppermute | solution.py:26
  155.3 4.7 %collective-permute-start.12 = (f32[2,5,8,64]{3,2,1,0:T(8,128)S(1)}, f32[2,5,8,64]{3,2,1,0:T(8,128)S(1)}, u32[]{:S(2)}, u32[]{:S(2)}) collective-permute-start(f32[2,5,8,64]{3,2,1,0:T(8,128)S(1)} %get-tuple-element.130), channel_id=1, source_target_pairs={{4,0},{8,4},{12,8},{16,12},{20,16},{24,20},{28,24},{5,1},{9,5},{13... | collective-permute-start | bytes 61448 | tf_op jit(solution)/shard_map/ppermute | solution.py:26
  160.1 6.0 %collective-permute-start.13 = (f32[2,18,5,64]{3,2,1,0:T(8,128)S(1)}, f32[2,18,5,64]{3,2,1,0:T(8,128)S(1)}, u32[]{:S(2)}, u32[]{:S(2)}) collective-permute-start(f32[2,18,5,64]{3,2,1,0:T(8,128)S(1)} %get-tuple-element.85), channel_id=1, source_target_pairs={{0,1},{1,2},{2,3},{4,5},{5,6},{6,7},{8,9},{9,10},{10,11},{12,13},{... | collective-permute-start | bytes 138248 | tf_op jit(solution)/shard_map/ppermute | solution.py:26
  164.1 6.5 %collective-permute-start.14 = (f32[2,18,5,64]{3,2,1,0:T(8,128)S(1)}, f32[2,18,5,64]{3,2,1,0:T(8,128)S(1)}, u32[]{:S(2)}, u32[]{:S(2)}) collective-permute-start(f32[2,18,5,64]{3,2,1,0:T(8,128)S(1)} %get-tuple-element.86), channel_id=1, source_target_pairs={{1,0},{2,1},{3,2},{5,4},{6,5},{7,6},{9,8},{10,9},{11,10},{13,12},{... | collective-permute-start | bytes 138248 | tf_op jit(solution)/shard_map/ppermute | solution.py:26
  172.3 1.1 copy-start.1
  172.3 1.3 copy-start.9
  (6 other events, 4.5 us)
